TPU v7x, 256 devices: a whole 4x4x8 slice. The times are simulated.
256 devices in a mesh: gx: 8 (over x, core), gy: 32 (over y, z).
Axes of the slice: x: 4, y: 4, z: 8, core: 2. Of those that a mesh axis runs over, the one named last changes fastest.
Arguments:
- hidden_in: bfloat16 [8192, 4096], P('gx', 'gy')
- norm_gain: bfloat16 [4096], P('gy'), may hold values from 0.099609375 to 1.8984375
- query_proj: bfloat16 [4096, 4096], P('gx', 'gy')
- kv_proj: bfloat16 [1024, 4096], P(None, 'gy')
- prompt_lengths: int32 [8], replicated, may hold values from 1 to 4096, 8192 in all
- cache_slot: int32 [512], replicated, may hold values from 0 to 511, as said below
Outputs:
- attention: bfloat16 [8192, 4096], P('gy', 'gx')
- kv_cache: bfloat16 [512, 16, 1024], P('gy', None, 'gx')
Inputs may be any that keep to these rules, and one draw needn't show every extreme that they name: `prompt_lengths`: the 8 prompts sum to 8192 tokens; the longest has exactly 4096. `cache_slot`: A permutation of the 512 slots; slot s is held by index s // 16 of gy. The 16 pages of one token block go to any one index at most 1 times, and every index receives exactly 16 pages.
All inputs are finite; a program needn't handle non-finite values.
Results may differ from a plain program's by a relative error of at most 0.0066.
The roundings to bfloat16 on the way count: a program that leaves them out, or rounds other values in their place, can miss the bound.
Values may be sent and summed in bfloat16 or wider, within the bound.
No kernel may reach another device: no remote copies, remote signals or barrier semaphores. Data moves between devices by JAX's collectives and lax.ppermute only.
A program may use at most 128 MiB of HBM per device.

v0:
```python
import math
import jax
import jax.numpy as jnp
from jax import lax
from jax.sharding import PartitionSpec as P

D = 4096
H = 32
KVH = 4
HD = 128
PAGES_DEV = 16
epsilon = 1e-06
rope_base = 5000000.0
masked_out = -1e30


def token_places(prompt_lengths, token_index):
    prompt_ends = jnp.cumsum(prompt_lengths)
    prompt_starts = prompt_ends - prompt_lengths
    segment = jnp.sum((token_index[:, None] >= prompt_ends[None, :]).astype(jnp.int32), axis=1)
    chosen = segment[:, None] == jnp.arange(prompt_lengths.shape[0], dtype=jnp.int32)[None, :]
    opening = jnp.sum(jnp.where(chosen, prompt_starts[None, :], 0), axis=1)
    return (segment, token_index - opening)


def rotate(vectors, places):
    half_size = vectors.shape[-1] // 2
    frequency = rope_base ** (-(jnp.arange(half_size, dtype=jnp.float32) * 2.0) / vectors.shape[-1])
    angles = places.astype(jnp.float32)[:, None] * frequency[None, :]
    cos_part = jnp.cos(angles)[:, None, :]
    sin_part = jnp.sin(angles)[:, None, :]
    leading = vectors[..., :half_size]
    trailing = vectors[..., half_size:]
    return jnp.concatenate(
        [leading * cos_part - trailing * sin_part, trailing * cos_part + leading * sin_part],
        axis=-1,
    )


def local(hidden_in, norm_gain, query_proj, kv_proj, prompt_lengths, cache_slot):
    count_gx = lax.axis_size("gx")
    count_gy = lax.axis_size("gy")
    where_gx = lax.axis_index("gx")
    where_gy = lax.axis_index("gy")
    local_rows = hidden_in.shape[0]
    block_tokens = local_rows * count_gx // count_gy
    all_tokens = block_tokens * count_gy
    heads_here = query_proj.shape[0] // HD
    group_size = H // KVH
    kv_head = where_gx * heads_here // group_size
    contract = (((1,), (1,)), ((), ()))
    kv_width = 2 * HD
    kv_start = kv_head * 2 * HD
    kv_rows = lax.dynamic_slice_in_dim(kv_proj, kv_start, kv_width, 0)
    widened = hidden_in.astype(jnp.float32)
    squares = jnp.sum(widened * widened, axis=1)
    totals = lax.psum(squares, "gy")
    normed = (
        widened * lax.rsqrt(totals / D + epsilon)[:, None] * norm_gain.astype(jnp.float32)[None, :]
    ).astype(jnp.bfloat16)
    gathered = lax.all_gather(normed, "gx", axis=0, tiled=True)
    stacked = jnp.concatenate([query_proj, kv_rows], axis=0)
    projected = lax.psum_scatter(
        lax.dot_general(gathered, stacked, contract, preferred_element_type=jnp.float32),
        "gy",
        scatter_dimension=0,
        tiled=True,
    )
    every_index = jnp.arange(all_tokens, dtype=jnp.int32)
    segment_all, place_all = token_places(prompt_lengths, every_index)
    first_query = where_gy * block_tokens
    token_index = first_query + jnp.arange(block_tokens, dtype=jnp.int32)
    segment_own = lax.dynamic_slice_in_dim(segment_all, first_query, block_tokens, 0)
    place_own = lax.dynamic_slice_in_dim(place_all, first_query, block_tokens, 0)
    query_cols = heads_here * HD
    queries = rotate(
        projected[:, :query_cols].reshape(block_tokens, heads_here, HD), place_own
    ).astype(jnp.bfloat16)
    keys = rotate(projected[:, query_cols : query_cols + HD][:, None, :], place_own)[
        :, 0, :
    ].astype(jnp.bfloat16)
    values = projected[:, query_cols + HD :].astype(jnp.bfloat16)
    cache_cols = jnp.where(where_gx % 2 == 0, keys, values)
    score_scale = 1.0 / math.sqrt(HD)
    last_query = first_query + block_tokens - 1
    first_segment = segment_own[0]
    initial = (
        jnp.full((heads_here, block_tokens), masked_out, jnp.float32),
        jnp.zeros((heads_here, block_tokens), jnp.float32),
        jnp.zeros((heads_here, block_tokens, HD), jnp.float32),
    )
    key_piece = lax.all_gather(keys, "gy", axis=0, tiled=True)
    value_piece = lax.all_gather(values, "gy", axis=0, tiled=True)
    block_count = key_piece.shape[0] // block_tokens
    key_blocks = key_piece.reshape(block_count, block_tokens, HD)
    value_blocks = value_piece.reshape(block_count, block_tokens, HD)

    def one_block(current, inputs):
        key_rows, value_rows, offset = inputs
        block_begin = offset * block_tokens
        key_segment = lax.dynamic_slice_in_dim(segment_all, block_begin, block_tokens, 0)
        skipped = jnp.logical_or(
            block_begin > last_query, key_segment[block_tokens - 1] < first_segment
        )

        def compute(previous):
            running_max, running_sum, running_acc = previous
            key_index = block_begin + jnp.arange(block_tokens, dtype=jnp.int32)
            allowed = (key_segment[None, :] == segment_own[:, None]) & (
                key_index[None, :] <= token_index[:, None]
            )
            scores = (
                jnp.einsum("qhd,kd->hqk", queries, key_rows, preferred_element_type=jnp.float32)
                * score_scale
            )
            scores = jnp.where(allowed[None], scores, masked_out)
            new_max = jnp.maximum(running_max, jnp.max(scores, axis=2))
            weights = jnp.where(allowed[None], jnp.exp(scores - new_max[..., None]), 0.0)
            factor = jnp.exp(running_max - new_max)
            new_sum = running_sum * factor + jnp.sum(weights, axis=2)
            update = jnp.einsum(
                "hqk,kd->hqd",
                weights.astype(jnp.bfloat16),
                value_rows,
                preferred_element_type=jnp.float32,
            )
            return (new_max, new_sum, running_acc * factor[..., None] + update)

        return (lax.cond(skipped, lambda previous: previous, compute, current), None)

    offsets = jnp.arange(block_count, dtype=jnp.int32)
    result, unused = lax.scan(one_block, initial, (key_blocks, value_blocks, offsets))
    final_max, final_sum, final_acc = result
    attention = (
        (final_acc / final_sum[..., None])
        .transpose(1, 0, 2)
        .reshape(block_tokens, query_cols)
        .astype(jnp.bfloat16)
    )
    pages_dev = PAGES_DEV
    page_len = block_tokens // pages_dev
    width_cols = cache_cols.shape[1]
    my_pages = cache_cols.reshape(pages_dev, page_len * width_cols)
    capacity = max(1, pages_dev // count_gy)
    slots_all = count_gy * capacity
    owners = (cache_slot // pages_dev).reshape(count_gy, pages_dev)
    page_range = jnp.arange(pages_dev, dtype=jnp.int32)
    earlier = page_range[None, :] < page_range[:, None]
    same_owner = owners[:, :, None] == owners[:, None, :]
    ranks = jnp.sum((same_owner & earlier[None]).astype(jnp.int32), axis=2)
    my_owner = lax.dynamic_index_in_dim(owners, where_gy, 0, keepdims=False)
    my_rank = lax.dynamic_index_in_dim(ranks, where_gy, 0, keepdims=False)
    target = my_owner * capacity + my_rank
    slot_range = jnp.arange(slots_all, dtype=jnp.int32)
    send_map = (slot_range[:, None] == target[None, :]).astype(jnp.bfloat16)
    outgoing = jnp.dot(send_map, my_pages, preferred_element_type=jnp.float32).astype(jnp.bfloat16)
    incoming = lax.all_to_all(outgoing, "gy", split_axis=0, concat_axis=0, tiled=True)
    wanted = where_gy * pages_dev + page_range
    matches = cache_slot[None, :] == wanted[:, None]
    page_ids = jnp.arange(cache_slot.shape[0], dtype=jnp.int32)
    source_page = jnp.sum(jnp.where(matches, page_ids[None, :], 0), axis=1)
    source_rank = jnp.sum(jnp.where(matches, ranks.reshape(-1)[None, :], 0), axis=1)
    source_slot = source_page // pages_dev * capacity + source_rank
    take_map = (source_slot[:, None] == slot_range[None, :]).astype(jnp.bfloat16)
    cache_block = jnp.dot(take_map, incoming, preferred_element_type=jnp.float32)
    cache_block = cache_block.astype(jnp.bfloat16).reshape(pages_dev, page_len, width_cols)
    return (attention, cache_block)


def solution(mesh):
    return jax.shard_map(
        local,
        mesh=mesh,
        in_specs=(P("gx", "gy"), P("gy"), P("gx", "gy"), P(None, "gy"), P(), P()),
        out_specs=(P("gy", "gx"), P("gy", None, "gx")),
        check_vma=False,
    )
```

profile of v0, /device:TPU:208, one launch (start us, length us, event | category | flops | bytes accessed | tf_op | source)
XLA Modules:
  0.0 692.0 jit_solution(10577667807313542377)
XLA Ops:
  7.2 1.2 fusion.19
  8.4 58.9 %psum.7 = f32[1024]{0:T(1024)S(1)} all-reduce(f32[1024]{0:T(1024)S(1)} %fusion.19), channel_id=1, replica_groups=mesh['gx'=8,'gy'=32] {'gy'}, use_global_device_ids=true, to_apply=%region_1.2 | all-reduce | flops 1024 | bytes 8192 | tf_op jit(solution)/shard_map/psum | solution.py:57
  67.9 1.9 fusion.21
  69.9 38.3 %all-gather.5.cloned.1.call-done = bf16[8192,128]{1,0:T(8,128)(2,1)} async-done(((bf16[1024,128]{1,0:T(8,128)(2,1)}), bf16[8192,128]{1,0:T(8,128)(2,1)}) %all-gather.5.cloned.1.call-update) | async-done | bytes 2097168 | tf_op jit(solution)/shard_map/all_gather | solution.py:61
  108.2 13.3 %fusion.23 = f32[8192,768]{0,1:T(8,128)} fusion(bf16[8192,128]{1,0:T(8,128)(2,1)} %all-gather.5.cloned.1.call-done, bf16[256,128]{1,0:T(8,128)(2,1)S(1)} %constant_dynamic-slice_fusion, bf16[512,128]{1,0:T(8,128)(2,1)} %param.12), kind=kOutput, calls=%fused_computation.42 | convolution fusion | flops 1611005952 | bytes 27459584 | tf_op jit(solution)/shard_map/dot_general | solution.py:64
  122.8 264.6 %reduce-scatter.2.cloned.1.call-done = f32[256,768]{0,1:T(8,128)} async-done(((f32[8192,768]{0,1:T(8,128)}), f32[256,768]{0,1:T(8,128)}) %reduce-scatter.2.cloned.1.call-update) | async-done | bytes 786448 | tf_op jit(solution)/shard_map/reduce_scatter | solution.py:63
  388.8 1.5 bitcast_select_fusion
  395.8 10.1 %all-to-all-start = ((bf16[32,2,1024]{2,1,0:T(2,128)(2,1)}), bf16[32,2,1024]{2,1,0:T(2,128)(2,1)S(1)}, u32[]{:S(2)}, u32[]{:S(2)}) async-start(bf16[32,2,1024]{2,1,0:T(2,128)(2,1)} %reshape.266), calls=%async_computation.1 | async-start | bytes 262144 | tf_op jit(solution)/shard_map/all_to_all | solution.py:157
  406.2 5.9 all-to-all-done
  413.1 52.7 %all-gather.7.cloned.1.call-done = bf16[8192,128]{0,1:T(8,128)(2,1)} async-done(((bf16[256,128]{0,1:T(8,128)(2,1)}), bf16[8192,128]{0,1:T(8,128)(2,1)}) %all-gather.7.cloned.1.call-update) | async-done | bytes 2097168 | tf_op jit(solution)/shard_map/all_gather | solution.py:93
  465.7 3.2 copy.72
  469.0 72.9 %all-gather.9.cloned.1.call-done = bf16[8192,1,128]{0,2,1:T(8,128)(2,1)} async-done(((bf16[256,1,128]{0,2,1:T(8,128)(2,1)}), bf16[8192,1,128]{0,2,1:T(8,128)(2,1)}) %all-gather.9.cloned.1.call-update) | async-done | bytes 2097168 | tf_op jit(solution)/shard_map/all_gather | solution.py:92
  541.8 4.1 copy.71
  546.0 138.6 %while.15 = (s32[]{:T(128)}, f32[4,256]{1,0:T(4,128)S(1)}, f32[4,256]{1,0:T(4,128)S(1)}, f32[4,256,128]{2,1,0:T(8,128)S(1)}, s32[32]{0:T(128)S(1)}, /*index=5*/s...) while((s32[]{:T(128)}, f32[4,256]{1,0:T(4,128)S(1)}, ...), condition=%wide.region_11.12_spmd.clone, body=%wide.region_6.11_spmd.clone.sunk | while | flops 137038352 | bytes 4926361 | solution.py:132
  568.6 2.1 conditional.3
  568.7 1.2 fusion.46
  573.9 2.1 conditional.3
  574.0 1.2 fusion.46
  579.2 2.1 conditional.3
  579.3 1.2 fusion.46
  584.5 2.1 conditional.3
  584.6 1.2 fusion.46
  589.8 2.1 conditional.3
  589.9 1.2 fusion.46
  595.1 2.1 conditional.3
  595.2 1.2 fusion.46
  600.4 2.1 conditional.3
  600.5 1.2 fusion.46
  605.7 2.1 conditional.3
  605.8 1.2 fusion.46
  611.0 2.1 conditional.3
  611.1 1.2 fusion.46
  616.3 2.1 conditional.3
  616.4 1.2 fusion.46
  621.6 2.1 conditional.3
  621.7 1.2 fusion.46
  626.9 2.1 conditional.3
  627.0 1.2 fusion.46
  632.2 2.1 conditional.3
  632.3 1.2 fusion.46
  637.5 2.1 conditional.3
  637.6 1.2 fusion.46
  642.8 2.1 conditional.3
  642.9 1.2 fusion.46
  648.1 2.1 conditional.3
  648.2 1.2 fusion.46
  653.4 2.1 conditional.3
  653.5 1.2 fusion.46
  (353 shorter events, 66.5 us)
Async XLA Ops:
  7.2 62.7 %copy-start = (bf16[1024,128]{1,0:T(8,128)(2,1)S(1)}, bf16[1024,128]{1,0:T(8,128)(2,1)}, u32[]{:S(2)}) copy-start(bf16[1024,128]{1,0:T(8,128)(2,1)} %param.13) | copy-start | bytes 786436
  7.2 101.1 %all-gather.5.cloned.1.call-start = ((), (), s32[]{:S(2)}) async-start(), calls=%async_computation.2 | async-start | bytes 2359296 | tf_op jit(solution)/shard_map/all_gather | solution.py:61
  69.8 317.6 %reduce-scatter.2.cloned.1.call-start = ((), (), s32[]{:S(2)}) async-start(), calls=%async_computation.3 | async-start | bytes 25952256 | tf_op jit(solution)/shard_map/reduce_scatter | solution.py:63
  121.6 0.7 copy-start.2
  121.6 270.1 %copy-start.1 = (s32[512]{0:T(512)S(1)}, s32[512]{0:T(512)}, u32[]{:S(2)}) copy-start(s32[512]{0:T(512)} %param.15) | copy-start | bytes 6148
  121.6 344.1 %all-gather.7.cloned.1.call-start = ((), (), s32[]{:S(2)}) async-start(), calls=%async_computation.4 | async-start | bytes 2162688 | tf_op jit(solution)/shard_map/all_gather | solution.py:93
  387.5 5.6 slice-start
  390.3 151.5 %all-gather.9.cloned.1.call-start = ((), (), s32[]{:S(2)}) async-start(), calls=%async_computation.5 | async-start | bytes 2162688 | tf_op jit(solution)/shard_map/all_gather | solution.py:92
  395.8 16.3 %all-to-all-start = ((bf16[32,2,1024]{2,1,0:T(2,128)(2,1)}), bf16[32,2,1024]{2,1,0:T(2,128)(2,1)S(1)}, u32[]{:S(2)}, u32[]{:S(2)}) async-start(bf16[32,2,1024]{2,1,0:T(2,128)(2,1)} %reshape.266), calls=%async_computation.1 | async-start | bytes 262144 | tf_op jit(solution)/shard_map/all_to_all | solution.py:157
Sparse Core Ops, SparseCore 0:
  69.9 38.2 all-gather.4
  121.7 265.7 reduce-scatter.1
  390.5 75.2 all-gather.6
  468.1 73.7 all-gather.8
where the time goes:
time: 694 us; the launch traced here: 692 us
  waiting for transfers between devices  434 us (63%)
  loops' own time  63.5 us (9%)
  blocking collectives  58.9 us (8%)
  local copies, waits for them, and re-layouts  52.8 us (8%)
  matrix products  42.2 us (6%)
  other arithmetic  16 us (2%)
  between operations  14 us (2%)
  starting transfers between devices  10.3 us (1%)
    reduce_scatter x1, waiting for transfers between devices, local(): lax.psum_scatter(lax.dot_general(gathered, stacked, contract, preferred_e...  265 us
    all_gather x1, waiting for transfers between devices, local(): key_piece = lax.all_gather(keys, 'gy', axis=0, tiled=True)  72.9 us
    another operation x1, loops' own time, local(): lax.scan(one_block, initial, (key_blocks, value_blocks, offsets))  62.1 us
    psum x1, blocking collectives, local(): totals = lax.psum(squares, 'gy')  58.9 us
    all_gather x1, waiting for transfers between devices, local(): value_piece = lax.all_gather(values, 'gy', axis=0, tiled=True)  52.7 us
    all_gather x1, waiting for transfers between devices, local(): gathered = lax.all_gather(normed, 'gx', axis=0, tiled=True)  38.3 us
    dot_general x17, matrix products, compute(): jnp.einsum('qhd,kd->hqk', queries, key_rows, preferred_element_type=jnp.f...  19.9 us
    slice x32, local copies, waits for them, and re-layouts, one_block(): key_segment[block_tokens - 1] < first_segment  18.9 us
  transfers between devices with their start and end apart: 5, of which 5 were waited for; matrix products, arithmetic and copies ran while one was open for 1% of the time, Pallas kernels for 0%

commit v1 on v0

--- a/solution.py
+++ b/solution.py
@@ -1,8 +1,10 @@
+import functools
 import math
 import jax
 import jax.numpy as jnp
 from jax import lax
 from jax.sharding import PartitionSpec as P
+from jax.lax import ppermute, psum
 
 D = 4096
 H = 32
@@ -12,6 +14,21 @@
 epsilon = 1e-06
 rope_base = 5000000.0
 masked_out = -1e30
+
+
+def _put_sums_all(z, net_axis):
+    sides = psum(1, axis_name=net_axis)
+    upper, raw_out = (z, 0)
+    while 1 << raw_out < sides:
+        odd = ppermute(
+            upper, axis_name=net_axis, perm=[(i, i ^ 1 << raw_out) for i in range(sides)]
+        )
+        upper = upper + odd
+        raw_out = raw_out + 1
+    return upper
+
+
+bind_teams_over_axis = functools.partial(_put_sums_all, net_axis="gy")
 
 
 def token_places(prompt_lengths, token_index):
@@ -54,7 +71,7 @@
     kv_rows = lax.dynamic_slice_in_dim(kv_proj, kv_start, kv_width, 0)
     widened = hidden_in.astype(jnp.float32)
     squares = jnp.sum(widened * widened, axis=1)
-    totals = lax.psum(squares, "gy")
+    totals = bind_teams_over_axis(squares)
     normed = (
         widened * lax.rsqrt(totals / D + epsilon)[:, None] * norm_gain.astype(jnp.float32)[None, :]
     ).astype(jnp.bfloat16)

time: 694 us -> 651 us (0.938)
  blocking collectives: 58.9 us -> 0 us
  waiting for transfers between devices: 434 us -> 444 us
    psum x1 -> x0, blocking collectives: 58.9 us -> none  [local(): totals = lax.psum(squares, 'gy')]
    ppermute x0 -> x5, waiting for transfers between devices: none -> 19 us  [_put_sums_all(): ppermute(upper, axis_name=net_axis, perm=[(i, i ^ 1 << raw_out) for i in...]
    all_gather x1, waiting for transfers between devices: 38.3 us -> 28.5 us  [local(): gathered = lax.all_gather(normed, 'gx', axis=0, tiled=True)]
  transfers between devices with their start and end apart: 5 -> 10, of which waited for: 5 -> 10; matrix products, arithmetic and copies ran while one was open for 1% -> 2% of each run, Pallas kernels for 0% -> 0%
where the time goes in v1:
time: 651 us; the launch traced here: 649 us
  waiting for transfers between devices  444 us (68%)
  loops' own time  65.2 us (10%)
  local copies, waits for them, and re-layouts  52.8 us (8%)
  matrix products  42.2 us (6%)
  other arithmetic  16 us (2%)
  starting transfers between devices  14.9 us (2%)
  between operations  14 us (2%)
    reduce_scatter x1, waiting for transfers between devices, local(): lax.psum_scatter(lax.dot_general(gathered, stacked, contract, preferred_e...  265 us
    all_gather x1, waiting for transfers between devices, local(): key_piece = lax.all_gather(keys, 'gy', axis=0, tiled=True)  72.9 us
    another operation x1, loops' own time, local(): lax.scan(one_block, initial, (key_blocks, value_blocks, offsets))  63.9 us
    all_gather x1, waiting for transfers between devices, local(): value_piece = lax.all_gather(values, 'gy', axis=0, tiled=True)  52.9 us
    all_gather x1, waiting for transfers between devices, local(): gathered = lax.all_gather(normed, 'gx', axis=0, tiled=True)  28.5 us
    dot_general x17, matrix products, compute(): jnp.einsum('qhd,kd->hqk', queries, key_rows, preferred_element_type=jnp.f...  19.9 us
    ppermute x5, waiting for transfers between devices, _put_sums_all(): ppermute(upper, axis_name=net_axis, perm=[(i, i ^ 1 << raw_out) for i in...  19 us
    slice x32, local copies, waits for them, and re-layouts, one_block(): key_segment[block_tokens - 1] < first_segment  18.9 us
  transfers between devices with their start and end apart: 10, of which 10 were waited for; matrix products, arithmetic and copies ran while one was open for 2% of the time, Pallas kernels for 0%

profile of v1, /device:TPU:208, one launch (start us, length us, event | category | flops | bytes accessed | tf_op | source)
XLA Modules:
  0.0 649.1 jit_solution(1689336288383197106)
XLA Ops:
  7.2 1.2 fusion.19
  9.5 2.6 collective-permute-done
  12.1 1.5 collective-permute-start.1
  13.6 3.1 collective-permute-done.1
  17.2 7.0 %collective-permute-done.2 = f32[1024]{0:T(1024)S(1)} collective-permute-done((f32[1024]{0:T(1024)S(1)}, f32[1024]{0:T(1024)S(1)}, u32[]{:S(2)}, u32[]{:S(2)}) %collective-permute-start.2) | collective-permute-done | bytes 4128 | tf_op jit(solution)/shard_map/ppermute | solution.py:23
  24.2 1.3 collective-permute-start.3
  25.4 2.3 collective-permute-done.3
  28.8 4.1 collective-permute-done.4
  32.9 1.9 fusion.21
  34.9 28.5 %all-gather.5.cloned.1.call-done = bf16[8192,128]{1,0:T(8,128)(2,1)} async-done(((bf16[1024,128]{1,0:T(8,128)(2,1)}), bf16[8192,128]{1,0:T(8,128)(2,1)}) %all-gather.5.cloned.1.call-update) | async-done | bytes 2097168 | tf_op jit(solution)/shard_map/all_gather | solution.py:78
  63.4 13.3 %fusion.23 = f32[8192,768]{0,1:T(8,128)} fusion(bf16[8192,128]{1,0:T(8,128)(2,1)} %all-gather.5.cloned.1.call-done, bf16[256,128]{1,0:T(8,128)(2,1)S(1)} %constant_dynamic-slice_fusion, bf16[512,128]{1,0:T(8,128)(2,1)} %param.12), kind=kOutput, calls=%fused_computation.42 | convolution fusion | flops 1611005952 | bytes 27459584 | tf_op jit(solution)/shard_map/dot_general | solution.py:81
  77.9 264.8 %reduce-scatter.2.cloned.1.call-done = f32[256,768]{0,1:T(8,128)} async-done(((f32[8192,768]{0,1:T(8,128)}), f32[256,768]{0,1:T(8,128)}) %reduce-scatter.2.cloned.1.call-update) | async-done | bytes 786448 | tf_op jit(solution)/shard_map/reduce_scatter | solution.py:80
  344.0 1.5 bitcast_select_fusion
  351.1 10.0 %all-to-all-start = ((bf16[32,2,1024]{2,1,0:T(2,128)(2,1)}), bf16[32,2,1024]{2,1,0:T(2,128)(2,1)S(1)}, u32[]{:S(2)}, u32[]{:S(2)}) async-start(bf16[32,2,1024]{2,1,0:T(2,128)(2,1)} %reshape.266), calls=%async_computation.1 | async-start | bytes 262144 | tf_op jit(solution)/shard_map/all_to_all | solution.py:174
  361.4 5.8 all-to-all-done
  368.2 52.9 %all-gather.7.cloned.1.call-done = bf16[8192,128]{0,1:T(8,128)(2,1)} async-done(((bf16[256,128]{0,1:T(8,128)(2,1)}), bf16[8192,128]{0,1:T(8,128)(2,1)}) %all-gather.7.cloned.1.call-update) | async-done | bytes 2097168 | tf_op jit(solution)/shard_map/all_gather | solution.py:110
  421.1 3.2 copy.72
  424.3 72.9 %all-gather.9.cloned.1.call-done = bf16[8192,1,128]{0,2,1:T(8,128)(2,1)} async-done(((bf16[256,1,128]{0,2,1:T(8,128)(2,1)}), bf16[8192,1,128]{0,2,1:T(8,128)(2,1)}) %all-gather.9.cloned.1.call-update) | async-done | bytes 2097168 | tf_op jit(solution)/shard_map/all_gather | solution.py:109
  497.2 4.1 copy.71
  501.3 140.3 %while.15 = (s32[]{:T(128)}, f32[4,256]{1,0:T(4,128)S(1)}, f32[4,256]{1,0:T(4,128)S(1)}, f32[4,256,128]{2,1,0:T(8,128)S(1)}, s32[32]{0:T(128)S(1)}, /*index=5*/s...) while((s32[]{:T(128)}, f32[4,256]{1,0:T(4,128)S(1)}, ...), condition=%wide.region_10.11_spmd.clone, body=%wide.region_5.10_spmd.clone.sunk | while | flops 137038352 | bytes 4926361 | solution.py:149
  524.3 2.1 conditional.3
  524.4 1.2 fusion.46
  529.6 2.1 conditional.3
  529.8 1.2 fusion.46
  535.0 2.1 conditional.3
  535.1 1.2 fusion.46
  540.3 2.1 conditional.3
  540.5 1.2 fusion.46
  545.7 2.1 conditional.3
  545.9 1.2 fusion.46
  551.0 2.1 conditional.3
  551.2 1.2 fusion.46
  556.4 2.1 conditional.3
  556.6 1.2 fusion.46
  561.8 2.1 conditional.3
  567.1 2.1 conditional.3
  572.5 2.1 conditional.3
  577.8 2.1 conditional.3
  578.0 1.2 fusion.46
  583.2 2.1 conditional.3
  588.5 2.1 conditional.3
  588.7 1.2 fusion.46
  593.9 2.1 conditional.3
  599.2 2.1 conditional.3
  599.4 1.2 fusion.46
  604.6 2.1 conditional.3
  610.0 2.1 conditional.3
  610.1 1.2 fusion.46
  (366 shorter events, 75.6 us)
Async XLA Ops:
  7.2 27.7 %copy-start = (bf16[1024,128]{1,0:T(8,128)(2,1)S(1)}, bf16[1024,128]{1,0:T(8,128)(2,1)}, u32[]{:S(2)}) copy-start(bf16[1024,128]{1,0:T(8,128)(2,1)} %param.13) | copy-start | bytes 786436
  7.2 56.2 %all-gather.5.cloned.1.call-start = ((), (), s32[]{:S(2)}) async-start(), calls=%async_computation.2 | async-start | bytes 2359296 | tf_op jit(solution)/shard_map/all_gather | solution.py:78
  8.4 3.7 collective-permute-start
  12.1 4.5 collective-permute-start.1
  16.6 7.5 %collective-permute-start.2 = (f32[1024]{0:T(1024)S(1)}, f32[1024]{0:T(1024)S(1)}, u32[]{:S(2)}, u32[]{:S(2)}) collective-permute-start(f32[1024]{0:T(1024)S(1)} %add.115), channel_id=1, source_target_pairs={{0,4},{1,5},{2,6},{3,7},{4,0},{5,1},{6,2},{7,3},{8,12},{9,13},{10,... | collective-permute-start | bytes 12296 | tf_op jit(solution)/shard_map/ppermute | solution.py:23
  24.2 3.6 collective-permute-start.3
  27.8 5.1 collective-permute-start.4
  34.8 308.0 %reduce-scatter.2.cloned.1.call-start = ((), (), s32[]{:S(2)}) async-start(), calls=%async_computation.3 | async-start | bytes 25952256 | tf_op jit(solution)/shard_map/reduce_scatter | solution.py:80
  76.7 0.7 copy-start.2
  76.7 270.3 %copy-start.1 = (s32[512]{0:T(512)S(1)}, s32[512]{0:T(512)}, u32[]{:S(2)}) copy-start(s32[512]{0:T(512)} %param.15) | copy-start | bytes 6148
  76.7 344.4 %all-gather.7.cloned.1.call-start = ((), (), s32[]{:S(2)}) async-start(), calls=%async_computation.4 | async-start | bytes 2162688 | tf_op jit(solution)/shard_map/all_gather | solution.py:110
  342.7 5.6 slice-start
  345.6 151.6 %all-gather.9.cloned.1.call-start = ((), (), s32[]{:S(2)}) async-start(), calls=%async_computation.5 | async-start | bytes 2162688 | tf_op jit(solution)/shard_map/all_gather | solution.py:109
  351.1 16.2 %all-to-all-start = ((bf16[32,2,1024]{2,1,0:T(2,128)(2,1)}), bf16[32,2,1024]{2,1,0:T(2,128)(2,1)S(1)}, u32[]{:S(2)}, u32[]{:S(2)}) async-start(bf16[32,2,1024]{2,1,0:T(2,128)(2,1)} %reshape.266), calls=%async_computation.1 | async-start | bytes 262144 | tf_op jit(solution)/shard_map/all_to_all | solution.py:174
Sparse Core Ops, SparseCore 0:
  34.9 28.4 all-gather.4
  76.8 265.8 reduce-scatter.1
  345.7 75.3 all-gather.6
  423.4 73.7 all-gather.8
